TPU v7x, 32 devices: a whole 2x2x4 slice. The times are simulated.
32 devices in a mesh: pair: 4 (over z), gen: 8 (over y, x, core).
Axes of the slice: x: 2, y: 2, z: 4, core: 2. Of those that a mesh axis runs over, the one named last changes fastest.
Arguments:
- tokens: bfloat16 [32768, 2048], P(('pair', 'gen')), may hold values from -6 to 6
- cotangent: bfloat16 [32768, 256], P(('pair', 'gen')), may hold values from -6 to 6
- block_pair: int32 [32, 1], replicated, may hold values from 0 to 15
- src_lang: int32 [16], replicated, may hold values from 0 to 95
- tgt_lang: int32 [16], replicated, may hold values from 0 to 95
- lang_embed: float32 [96, 512], P(None, 'pair'), may hold values from -5 to 5
- generator: bfloat16 [512, 524288], P('pair', 'gen'), may hold values from -0.005859375 to 0.005859375
Outputs:
- grad_tokens: bfloat16 [32768, 2048], P(('pair', 'gen'))
- grad_generator: bfloat16 [512, 524288], P('pair', 'gen')
- grad_embed: float32 [96, 512], P(None, 'pair')
Inputs may be any that keep to these rules, and one draw needn't show every extreme that they name: `block_pair`: every pair owns at least one block; block counts per pair are uneven.
All inputs are finite; a program needn't handle non-finite values.
Results may differ from a plain program's by a relative error of at most 0.007.
Values may be sent and summed in bfloat16 or wider, within the bound.
No kernel may reach another device: no remote copies, remote signals or barrier semaphores. Data moves between devices by JAX's collectives and lax.ppermute only.
A program may use at most 128 MiB of HBM per device.

v0:
```python
import jax
import jax.numpy as jnp
from jax import lax
from jax.sharding import PartitionSpec as P

BLK = 1024


def shards(tokens, cotangent, block_pair, src_lang, tgt_lang, lang_embed, generator):
    gen_count = lax.axis_size("gen")
    pair_count_axis = lax.axis_size("pair")
    blocks_here = tokens.shape[0] // BLK
    model_width = tokens.shape[1]
    adapter_rank = cotangent.shape[1]
    languages = lang_embed.shape[0]
    pair_count = src_lang.shape[0]
    chunk = generator.shape[1]
    quarter = chunk // pair_count_axis
    lang_ids = jnp.arange(languages, dtype=jnp.int32)
    hot_both = (src_lang[:, None] == lang_ids[None, :]).astype(jnp.float32) + (
        tgt_lang[:, None] == lang_ids[None, :]
    ).astype(jnp.float32)
    pair_embed = jnp.dot(hot_both, lang_embed, precision=lax.Precision.HIGHEST).astype(jnp.bfloat16)
    partial_value = jnp.dot(pair_embed, generator, preferred_element_type=jnp.float32)
    adapter_part = lax.psum_scatter(
        partial_value.astype(jnp.bfloat16), "pair", scatter_dimension=1, tiled=True
    )
    flat_pairs = block_pair[:, 0]
    outgoing = jnp.take(adapter_part, flat_pairs, axis=0)
    incoming = lax.all_to_all(outgoing, ("pair", "gen"), 0, 0, tiled=True)
    adapters = (
        incoming.reshape(pair_count_axis, gen_count, quarter)
        .transpose(1, 0, 2)
        .reshape(blocks_here, model_width, adapter_rank)
    )
    token_blocks = tokens.reshape(blocks_here, BLK, model_width)
    cot_blocks = cotangent.reshape(blocks_here, BLK, adapter_rank)
    hidden = jnp.einsum("btd,bdr->btr", token_blocks, adapters, preferred_element_type=jnp.float32)
    logistic = jax.nn.sigmoid(hidden)
    grad_hidden = (
        cot_blocks.astype(jnp.float32) * logistic * (1.0 + hidden * (1.0 - logistic))
    ).astype(jnp.bfloat16)
    grad_tokens = (
        jnp.einsum("btr,bdr->btd", grad_hidden, adapters, preferred_element_type=jnp.float32)
        .astype(jnp.bfloat16)
        .reshape(tokens.shape)
    )
    outer_grads = jnp.einsum(
        "btd,btr->bdr", token_blocks, grad_hidden, preferred_element_type=jnp.float32
    )
    by_owner = (
        outer_grads.reshape(gen_count, pair_count_axis, quarter)
        .transpose(1, 0, 2)
        .reshape(pair_count_axis * gen_count, quarter)
        .astype(jnp.bfloat16)
    )
    returned = lax.all_to_all(by_owner, ("pair", "gen"), 0, 0, tiled=True)
    pair_ids = jnp.arange(pair_count, dtype=jnp.int32)
    segment_hot = (pair_ids[:, None] == flat_pairs[None, :]).astype(jnp.float32)
    row_grad = jnp.dot(
        segment_hot, returned.astype(jnp.float32), precision=lax.Precision.HIGHEST
    ).astype(jnp.bfloat16)
    grad_rounded = lax.all_gather(row_grad, "pair", axis=1, tiled=True)
    grad_generator = jnp.einsum(
        "pe,pc->ec", pair_embed, grad_rounded, preferred_element_type=jnp.float32
    ).astype(jnp.bfloat16)
    partial_pair = jnp.einsum(
        "pc,ec->pe", grad_rounded, generator, preferred_element_type=jnp.float32
    )
    grad_pair = lax.psum(partial_pair, "gen")
    grad_embed = jnp.dot(hot_both.T, grad_pair, precision=lax.Precision.HIGHEST)
    return (grad_tokens, grad_generator, grad_embed)


def solution(mesh):
    placed = (
        P(("pair", "gen"), None),
        P(("pair", "gen"), None),
        P(),
        P(),
        P(),
        P(None, "pair"),
        P("pair", "gen"),
    )
    return jax.shard_map(
        shards,
        mesh=mesh,
        in_specs=placed,
        out_specs=(P(("pair", "gen"), None), P("pair", "gen"), P(None, "pair")),
        check_vma=False,
    )
```

profile of v0, /device:TPU:0, one launch (start us, length us, event | category | flops | bytes accessed | tf_op | source)
XLA Modules:
  0.0 235.5 jit_solution(6820055431846227179)
XLA Ops:
  8.0 0.9 convolution_convert_fusion.5
  8.9 9.4 %convolution_convert_fusion.1 = bf16[16,65536]{1,0:T(8,128)(2,1)} fusion(bf16[16,128]{1,0:T(8,128)(2,1)S(1)} %convolution_convert_fusion.5, bf16[128,65536]{1,0:T(8,128)(2,1)} %param.13), kind=kOutput, calls=%fused_computation.2 | convolution fusion | flops 269484032 | bytes 18878464 | tf_op jit(solution)/shard_map/dot_general | solution.py:24
  18.3 46.7 %reduce-scatter.2.cloned.1.call-done = bf16[16,16384]{1,0:T(8,128)(2,1)} async-done(((bf16[16,65536]{1,0:T(8,128)(2,1)}), bf16[16,16384]{1,0:T(8,128)(2,1)}) %reduce-scatter.2.cloned.1.call-update) | async-done | bytes 524304 | tf_op jit(solution)/shard_map/reduce_scatter | solution.py:25
  65.0 3.2 %gather_fusion = bf16[32,16384]{1,0:T(8,128)(2,1)S(1)} fusion(bf16[16,16384]{1,0:T(8,128)(2,1)} %reduce-scatter.2.cloned.1.call-done, s32[1024]{0:T(1024)S(1)} %pad_clamp_fusion), kind=kCustom, calls=%fused_computation | custom fusion | bytes 2097280 | tf_op jit(solution)/shard_map/jit(_take)/gather | solution.py:29
  68.9 1.4 reduce
  70.4 1.6 reshape.111
  72.0 3.9 %all-to-all-start = ((bf16[32,2,8192]{2,1,0:T(2,128)(2,1)}), bf16[32,2,8192]{2,1,0:T(2,128)(2,1)S(1)}, u32[]{:S(2)}, u32[]{:S(2)}) async-start(bf16[32,2,8192]{2,1,0:T(2,128)(2,1)} %reshape.111), calls=%async_computation.1 | async-start | bytes 2097152 | tf_op jit(solution)/shard_map/all_to_all | solution.py:30
  76.1 1.0 copy.21
  77.1 25.0 %all-to-all-done = bf16[32,2,8192]{2,1,0:T(2,128)(2,1)S(1)} async-done(((bf16[32,2,8192]{2,1,0:T(2,128)(2,1)}), bf16[32,2,8192]{2,1,0:T(2,128)(2,1)S(1)}, u32[]{:S(2)}, u32[]{:S(2)}) %all-to-all-start) | async-done | bytes 1048608 | tf_op jit(solution)/shard_map/all_to_all | solution.py:30
  102.1 1.0 reshape.112
  103.2 1.2 copy.35
  105.9 3.9 %convolution_bitcast_fusion = f32[1024,256]{0,1:T(8,128)S(1)} fusion(bf16[2048,256]{1,0:T(8,128)(2,1)S(1)} %reshape.102, bf16[1024,2048]{1,0:T(8,128)(2,1)} %param.7), kind=kOutput, calls=%fused_computation.7 | convolution fusion | flops 1073741824 | bytes 6291456 | tf_op jit(solution)/shard_map/btd,bdr->btr/dot_general | solution.py:38
  109.9 1.0 copy-done.10
  110.8 1.5 fusion
  114.3 1.4 reduce.1
  116.5 29.7 %all_to_all.15 = bf16[32,2,8192]{2,1,0:T(2,128)(2,1)S(1)} all-to-all(bf16[32,2,8192]{2,1,0:T(2,128)(2,1)S(1)} %reshape.113), channel_id=1, replica_groups=mesh['pair'=4,'gen'=8] {'pair','gen'}, dimensions={0} | all-to-all | bytes 2097152 | tf_op jit(solution)/shard_map/all_to_all | solution.py:57
  146.2 1.0 reshape.114
  147.3 2.0 convolution_convert_fusion.2
  149.3 5.3 %convolution_convert_fusion.3 = bf16[1024,2048]{1,0:T(8,128)(2,1)} fusion(bf16[2048,256]{1,0:T(8,128)(2,1)} %copy-done.3, f32[1024,256]{0,1:T(8,128)} %copy-done.10, bf16[1024,256]{0,1:T(8,128)(2,1)} %copy.21), kind=kOutput, calls=%fused_computation.4 | convolution fusion | flops 1078460416 | bytes 6815744 | tf_op jit(solution)/shard_map/btr,bdr->btd/dot_general | solution.py:44
  154.6 39.8 %all-gather.2.cloned.1.call-done = bf16[16,65536]{1,0:T(8,128)(2,1)} async-done(((bf16[16,16384]{1,0:T(8,128)(2,1)}), bf16[16,65536]{1,0:T(8,128)(2,1)}) %all-gather.2.cloned.1.call-update) | async-done | bytes 2097168 | tf_op jit(solution)/shard_map/all_gather | solution.py:63
  194.4 11.0 %fusion.16 = f32[16,128]{1,0:T(8,128)S(1)} fusion(bf16[16,65536]{1,0:T(8,128)(2,1)} %all-gather.2.cloned.1.call-done, bf16[128,65536]{1,0:T(8,128)(2,1)} %param.13), kind=kOutput, calls=%fused_computation.35 | convolution fusion | flops 268435456 | bytes 18882560 | tf_op jit(solution)/shard_map/pc,ec->pe/dot_general | solution.py:67
  205.4 13.8 %psum.7 = f32[16,128]{1,0:T(8,128)S(1)} all-reduce(f32[16,128]{1,0:T(8,128)S(1)} %fusion.16), channel_id=1, replica_groups=mesh['pair'=4,'gen'=8] {'gen'}, use_global_device_ids=true, to_apply=%region_1.2 | all-reduce | flops 2048 | bytes 16384 | tf_op jit(solution)/shard_map/psum | solution.py:70
  219.2 1.0 fusion.7
  220.2 8.5 %convolution_convert_fusion = bf16[128,65536]{1,0:T(8,128)(2,1)} fusion(bf16[16,128]{1,0:T(8,128)(2,1)S(1)} %convolution_convert_fusion.5, bf16[16,65536]{1,0:T(8,128)(2,1)S(1)} %copy-done.2), kind=kOutput, calls=%fused_computation.1 | convolution fusion | flops 276824064 | bytes 18878464 | tf_op jit(solution)/shard_map/pe,pc->ec/dot_general | solution.py:64
  (36 shorter events, 6.1 us)
Async XLA Ops:
  7.2 0.8 copy-start
  7.2 57.8 %reduce-scatter.2.cloned.1.call-start = ((), (), s32[]{:S(2)}) async-start(), calls=%async_computation.3 | async-start | bytes 2621440 | tf_op jit(solution)/shard_map/reduce_scatter | solution.py:25
  8.8 9.4 %copy-start.6 = (s32[32,1]{0,1:T(1,128)S(1)}, s32[32,1]{0,1:T(1,128)}, u32[]{:S(2)}) copy-start(s32[32,1]{0,1:T(1,128)} %param.9) | copy-start | bytes 388
  68.2 7.9 %copy-start.4 = (bf16[1024,256]{1,0:T(8,128)(2,1)S(1)}, bf16[1024,256]{1,0:T(8,128)(2,1)}, u32[]{:S(2)}) copy-start(bf16[1024,256]{1,0:T(8,128)(2,1)} %param.8) | copy-start | bytes 1572868
  72.0 30.1 %all-to-all-start = ((bf16[32,2,8192]{2,1,0:T(2,128)(2,1)}), bf16[32,2,8192]{2,1,0:T(2,128)(2,1)S(1)}, u32[]{:S(2)}, u32[]{:S(2)}) async-start(bf16[32,2,8192]{2,1,0:T(2,128)(2,1)} %reshape.111), calls=%async_computation.1 | async-start | bytes 2097152 | tf_op jit(solution)/shard_map/all_to_all | solution.py:30
  75.9 118.5 %all-gather.2.cloned.1.call-start = ((), (), s32[]{:S(2)}) async-start(), calls=%async_computation.4 | async-start | bytes 2621440 | tf_op jit(solution)/shard_map/all_gather | solution.py:63
  105.9 6.4 %copy-start.3 = (bf16[2048,256]{1,0:T(8,128)(2,1)}, bf16[2048,256]{1,0:T(8,128)(2,1)S(1)}, u32[]{:S(2)}) copy-start(bf16[2048,256]{1,0:T(8,128)(2,1)S(1)} %reshape.102) | copy-start | bytes 3145732
  105.9 4.9 %copy-start.5 = (bf16[1024,256]{0,1:T(8,128)(2,1)S(1)}, bf16[1024,256]{0,1:T(8,128)(2,1)}, u32[]{:S(2)}) copy-start(bf16[1024,256]{0,1:T(8,128)(2,1)} %copy.21) | copy-start | bytes 1572868
  105.9 4.9 %copy-start.7 = (bf16[1024,2048]{1,0:T(8,128)(2,1)S(1)}, bf16[1024,2048]{1,0:T(8,128)(2,1)}, u32[]{:S(2)}) copy-start(bf16[1024,2048]{1,0:T(8,128)(2,1)} %param.7) | copy-start | bytes 12582916
  109.8 1.0 copy-start.10
  154.6 64.6 %copy-start.8 = (s32[16]{0:T(128)S(1)}, s32[16]{0:T(128)}, u32[]{:S(2)}) copy-start(s32[16]{0:T(128)} %param.11) | copy-start | bytes 196
  154.6 64.6 %copy-start.9 = (s32[16]{0:T(128)S(1)}, s32[16]{0:T(128)}, u32[]{:S(2)}) copy-start(s32[16]{0:T(128)} %param.10) | copy-start | bytes 196
  194.4 25.8 %copy-start.2 = (bf16[16,65536]{1,0:T(8,128)(2,1)S(1)}, bf16[16,65536]{1,0:T(8,128)(2,1)}, u32[]{:S(2)}) copy-start(bf16[16,65536]{1,0:T(8,128)(2,1)} %all-gather.2.cloned.1.call-done) | copy-start | bytes 6291460
  220.2 8.5 %copy-start.1 = (f32[96,128]{1,0:T(8,128)S(1)}, f32[96,128]{1,0:T(8,128)}, u32[]{:S(2)}) copy-start(f32[96,128]{1,0:T(8,128)} %param.12) | copy-start | bytes 147460
Sparse Core Ops, SparseCore 0:
  18.4 46.5 reduce-scatter.1
  149.4 44.9 all-gather.1
where the time goes:
time: 236 us
  waiting for transfers between devices  111 us (47%)
  blocking collectives  43.5 us (18%)
  matrix products  43.4 us (18%)
  local copies, waits for them, and re-layouts  15.6 us (7%)
  between operations  14.3 us (6%)
  starting transfers between devices  4.17 us (2%)
  other arithmetic  3.07 us (1%)
    reduce_scatter x1, waiting for transfers between devices, shards(): lax.psum_scatter(partial_value.astype(jnp.bfloat16), 'pair', scatter_dime...  46.7 us
    all_gather x1, waiting for transfers between devices, shards(): grad_rounded = lax.all_gather(row_grad, 'pair', axis=1, tiled=True)  39.8 us
    all_to_all x1, blocking collectives, shards(): returned = lax.all_to_all(by_owner, ('pair', 'gen'), 0, 0, tiled=True)  29.7 us
    all_to_all x1, waiting for transfers between devices, shards(): incoming = lax.all_to_all(outgoing, ('pair', 'gen'), 0, 0, tiled=True)  25 us
    psum x1, blocking collectives, shards(): grad_pair = lax.psum(partial_pair, 'gen')  13.8 us
    dot_general x1, matrix products, shards(): jnp.einsum('pc,ec->pe', grad_rounded, generator, preferred_element_type=j...  11 us
    dot_general x1, matrix products, shards(): jnp.dot(pair_embed, generator, preferred_element_type=jnp.float32)  9.4 us
    dot_general x1, matrix products, shards(): jnp.einsum('pe,pc->ec', pair_embed, grad_rounded, preferred_element_type=...  8.52 us
  transfers between devices with their start and end apart: 3, of which 3 were waited for; matrix products, arithmetic and copies ran while one was open for 3% of the time, Pallas kernels for 0%

commit v1 on v0

--- a/solution.py
+++ b/solution.py
@@ -60,7 +60,9 @@
     row_grad = jnp.dot(
         segment_hot, returned.astype(jnp.float32), precision=lax.Precision.HIGHEST
     ).astype(jnp.bfloat16)
-    grad_rounded = lax.all_gather(row_grad, "pair", axis=1, tiled=True)
+    grad_rounded = jnp.concatenate(
+        lax.all_to_all(jnp.stack([row_grad] * lax.axis_size("pair")), "pair", 0, 0), axis=1
+    )
     grad_generator = jnp.einsum(
         "pe,pc->ec", pair_embed, grad_rounded, preferred_element_type=jnp.float32
     ).astype(jnp.bfloat16)

time: 236 us -> 243 us (1.030)
  local copies, waits for them, and re-layouts: 15.6 us -> 20.1 us
  matrix products: 43.4 us -> 39.5 us
  starting transfers between devices: 4.17 us -> 7.95 us
  waiting for transfers between devices: 111 us -> 114 us
    all_to_all x0 -> x1, waiting for transfers between devices: none -> 42.7 us  [shards(): lax.all_to_all(jnp.stack([row_grad] * lax.axis_size('pair')), 'pair', 0, 0)]
    all_gather x1 -> x0, waiting for transfers between devices: 39.8 us -> none  [shards(): grad_rounded = lax.all_gather(row_grad, 'pair', axis=1, tiled=True)]
    all_to_all x0 -> x1, starting transfers between devices: none -> 3.83 us  [shards(): lax.all_to_all(jnp.stack([row_grad] * lax.axis_size('pair')), 'pair', 0, 0)]
    dot_general x1, matrix products: 11 us -> 8.06 us  [shards(): jnp.einsum('pc,ec->pe', grad_rounded, generator, preferred_element_type=j...]
    unnamed x28 -> x30, local copies, waits for them, and re-layouts: 8.39 us -> 9.71 us
  transfers between devices with their start and end apart: 3 -> 3, of which waited for: 3 -> 3; matrix products, arithmetic and copies ran while one was open for 3% -> 2% of each run, Pallas kernels for 0% -> 0%
where the time goes in v1:
time: 243 us; the launch traced here: 242 us
  waiting for transfers between devices  114 us (47%)
  blocking collectives  42.8 us (18%)
  matrix products  39.5 us (16%)
  local copies, waits for them, and re-layouts  20.1 us (8%)
  between operations  14.3 us (6%)
  starting transfers between devices  7.95 us (3%)
  other arithmetic  3.07 us (1%)
    reduce_scatter x1, waiting for transfers between devices, shards(): lax.psum_scatter(partial_value.astype(jnp.bfloat16), 'pair', scatter_dime...  46.7 us
    all_to_all x1, waiting for transfers between devices, shards(): lax.all_to_all(jnp.stack([row_grad] * lax.axis_size('pair')), 'pair', 0, 0)  42.7 us
    all_to_all x1, blocking collectives, shards(): returned = lax.all_to_all(by_owner, ('pair', 'gen'), 0, 0, tiled=True)  29.7 us
    all_to_all x1, waiting for transfers between devices, shards(): incoming = lax.all_to_all(outgoing, ('pair', 'gen'), 0, 0, tiled=True)  25 us
    psum x1, blocking collectives, shards(): grad_pair = lax.psum(partial_pair, 'gen')  13.2 us
    unnamed x30, local copies, waits for them, and re-layouts  9.71 us
    dot_general x1, matrix products, shards(): jnp.dot(pair_embed, generator, preferred_element_type=jnp.float32)  9.4 us
    dot_general x1, matrix products, shards(): jnp.einsum('pe,pc->ec', pair_embed, grad_rounded, preferred_element_type=...  8.55 us
  transfers between devices with their start and end apart: 3, of which 3 were waited for; matrix products, arithmetic and copies ran while one was open for 2% of the time, Pallas kernels for 0%

profile of v1, /device:TPU:0, one launch (start us, length us, event | category | flops | bytes accessed | tf_op | source)
XLA Modules:
  0.0 242.2 jit_solution(1088679371082069394)
XLA Ops:
  8.9 9.4 %convolution_convert_fusion.1 = bf16[16,65536]{1,0:T(8,128)(2,1)} fusion(bf16[16,128]{1,0:T(8,128)(2,1)S(1)} %convolution_convert_fusion.5, bf16[128,65536]{1,0:T(8,128)(2,1)} %param.13), kind=kOutput, calls=%fused_computation.2 | convolution fusion | flops 269484032 | bytes 18878464 | tf_op jit(solution)/shard_map/dot_general | solution.py:24
  18.3 46.7 %reduce-scatter.2.cloned.1.call-done = bf16[16,16384]{1,0:T(8,128)(2,1)} async-done(((bf16[16,65536]{1,0:T(8,128)(2,1)}), bf16[16,16384]{1,0:T(8,128)(2,1)}) %reduce-scatter.2.cloned.1.call-update) | async-done | bytes 524304 | tf_op jit(solution)/shard_map/reduce_scatter | solution.py:25
  65.0 3.2 %gather_fusion = bf16[32,16384]{1,0:T(8,128)(2,1)S(1)} fusion(bf16[16,16384]{1,0:T(8,128)(2,1)} %reduce-scatter.2.cloned.1.call-done, s32[1024]{0:T(1024)S(1)} %pad_clamp_fusion), kind=kCustom, calls=%fused_computation | custom fusion | bytes 2097280 | tf_op jit(solution)/shard_map/jit(_take)/gather | solution.py:29
  68.9 1.4 reduce
  70.4 1.6 reshape.121
  72.0 4.1 %all-to-all-start = ((bf16[32,2,8192]{2,1,0:T(2,128)(2,1)}), bf16[32,2,8192]{2,1,0:T(2,128)(2,1)S(1)}, u32[]{:S(2)}, u32[]{:S(2)}) async-start(bf16[32,2,8192]{2,1,0:T(2,128)(2,1)} %reshape.121), calls=%async_computation.1 | async-start | bytes 2097152 | tf_op jit(solution)/shard_map/all_to_all | solution.py:30
  77.1 25.0 %all-to-all-done = bf16[32,2,8192]{2,1,0:T(2,128)(2,1)S(1)} async-done(((bf16[32,2,8192]{2,1,0:T(2,128)(2,1)}), bf16[32,2,8192]{2,1,0:T(2,128)(2,1)S(1)}, u32[]{:S(2)}, u32[]{:S(2)}) %all-to-all-start) | async-done | bytes 1048608 | tf_op jit(solution)/shard_map/all_to_all | solution.py:30
  102.1 1.0 reshape.122
  103.2 1.2 copy.38
  105.9 3.9 %convolution_bitcast_fusion = f32[1024,256]{0,1:T(8,128)S(1)} fusion(bf16[2048,256]{1,0:T(8,128)(2,1)S(1)} %reshape.110, bf16[1024,2048]{1,0:T(8,128)(2,1)} %param.7), kind=kOutput, calls=%fused_computation.7 | convolution fusion | flops 1073741824 | bytes 6291456 | tf_op jit(solution)/shard_map/btd,bdr->btr/dot_general | solution.py:38
  110.8 1.5 fusion
  114.3 1.4 reduce.1
  116.6 29.7 %all_to_all.20 = bf16[32,2,8192]{2,1,0:T(2,128)(2,1)S(1)} all-to-all(bf16[32,2,8192]{2,1,0:T(2,128)(2,1)S(1)} %reshape.123), channel_id=1, replica_groups=mesh['pair'=4,'gen'=8] {'pair','gen'}, dimensions={0} | all-to-all | bytes 2097152 | tf_op jit(solution)/shard_map/all_to_all | solution.py:57
  146.2 1.0 reshape.124
  147.3 1.2 convolution_convert_fusion.2
  148.5 1.5 stack.2
  150.0 3.8 %all-to-all-start.2 = ((bf16[4,16,16384]{2,1,0:T(8,128)(2,1)}), bf16[4,16,16384]{2,1,0:T(8,128)(2,1)S(1)}, u32[]{:S(2)}, u32[]{:S(2)}) async-start(bf16[4,16,16384]{2,1,0:T(8,128)(2,1)} %stack.2), calls=%async_computation.3 | async-start | bytes 4194304 | tf_op jit(solution)/shard_map/all_to_all | solution.py:64
  153.8 5.0 %convolution_convert_fusion.3 = bf16[1024,2048]{1,0:T(8,128)(2,1)} fusion(bf16[2048,256]{1,0:T(8,128)(2,1)S(1)} %copy-done.4, f32[1024,256]{0,1:T(8,128)} %copy-done.11, bf16[1024,256]{0,1:T(8,128)(2,1)} %copy.22), kind=kOutput, calls=%fused_computation.4 | convolution fusion | flops 1078460416 | bytes 6815744 | tf_op jit(solution)/shard_map/btr,bdr->btd/dot_general | solution.py:44
  158.8 42.7 %all-to-all-done.2 = bf16[4,16,16384]{2,1,0:T(8,128)(2,1)S(1)} async-done(((bf16[4,16,16384]{2,1,0:T(8,128)(2,1)}), bf16[4,16,16384]{2,1,0:T(8,128)(2,1)S(1)}, u32[]{:S(2)}, u32[]{:S(2)}) %all-to-all-start.2) | async-done | bytes 2097184 | tf_op jit(solution)/shard_map/all_to_all | solution.py:64
  201.5 1.3 copy-done.2
  202.8 1.7 copy.31
  204.6 8.5 %convolution_convert_fusion = bf16[128,65536]{1,0:T(8,128)(2,1)} fusion(bf16[16,128]{1,0:T(8,128)(2,1)S(1)} %convolution_convert_fusion.5, bf16[16,65536]{1,0:T(8,128)(2,1)S(1)} %bitcast.38), kind=kOutput, calls=%fused_computation.1 | convolution fusion | flops 276824064 | bytes 18878464 | tf_op jit(solution)/shard_map/pe,pc->ec/dot_general | solution.py:66
  213.1 8.1 %fusion.16 = f32[16,128]{1,0:T(8,128)S(1)} fusion(bf16[16,65536]{1,0:T(8,128)(2,1)S(1)} %bitcast.39, bf16[128,65536]{1,0:T(8,128)(2,1)} %param.13), kind=kOutput, calls=%fused_computation.35 | convolution fusion | flops 268435456 | bytes 18882560 | tf_op jit(solution)/shard_map/pc,ec->pe/dot_general | solution.py:69
  221.2 13.2 %psum.7 = f32[16,128]{1,0:T(8,128)S(1)} all-reduce(f32[16,128]{1,0:T(8,128)S(1)} %fusion.16), channel_id=1, replica_groups=mesh['pair'=4,'gen'=8] {'gen'}, use_global_device_ids=true, to_apply=%region_1.2 | all-reduce | flops 2048 | bytes 16384 | tf_op jit(solution)/shard_map/psum | solution.py:72
  (39 shorter events, 9.7 us)
Async XLA Ops:
  7.2 0.8 copy-start
  7.2 57.8 %reduce-scatter.2.cloned.1.call-start = ((), (), s32[]{:S(2)}) async-start(), calls=%async_computation.4 | async-start | bytes 2621440 | tf_op jit(solution)/shard_map/reduce_scatter | solution.py:25
  8.8 9.4 %copy-start.7 = (s32[32,1]{0,1:T(1,128)S(1)}, s32[32,1]{0,1:T(1,128)}, u32[]{:S(2)}) copy-start(s32[32,1]{0,1:T(1,128)} %param.9) | copy-start | bytes 388
  68.2 7.8 %copy-start.5 = (bf16[1024,256]{1,0:T(8,128)(2,1)S(1)}, bf16[1024,256]{1,0:T(8,128)(2,1)}, u32[]{:S(2)}) copy-start(bf16[1024,256]{1,0:T(8,128)(2,1)} %param.8) | copy-start | bytes 1572868
  72.0 30.2 %all-to-all-start = ((bf16[32,2,8192]{2,1,0:T(2,128)(2,1)}), bf16[32,2,8192]{2,1,0:T(2,128)(2,1)S(1)}, u32[]{:S(2)}, u32[]{:S(2)}) async-start(bf16[32,2,8192]{2,1,0:T(2,128)(2,1)} %reshape.121), calls=%async_computation.1 | async-start | bytes 2097152 | tf_op jit(solution)/shard_map/all_to_all | solution.py:30
  105.9 6.5 %copy-start.3 = (bf16[2048,256]{1,0:T(8,128)(2,1)}, bf16[2048,256]{1,0:T(8,128)(2,1)S(1)}, u32[]{:S(2)}) copy-start(bf16[2048,256]{1,0:T(8,128)(2,1)S(1)} %reshape.110) | copy-start | bytes 3145732
  105.9 4.9 %copy-start.6 = (bf16[1024,256]{0,1:T(8,128)(2,1)S(1)}, bf16[1024,256]{0,1:T(8,128)(2,1)}, u32[]{:S(2)}) copy-start(bf16[1024,256]{0,1:T(8,128)(2,1)} %copy.22) | copy-start | bytes 1572868
  105.9 4.9 %copy-start.8 = (bf16[1024,2048]{1,0:T(8,128)(2,1)S(1)}, bf16[1024,2048]{1,0:T(8,128)(2,1)}, u32[]{:S(2)}) copy-start(bf16[1024,2048]{1,0:T(8,128)(2,1)} %param.7) | copy-start | bytes 12582916
  109.8 1.0 copy-start.11
  147.3 6.5 %copy-start.4 = (bf16[2048,256]{1,0:T(8,128)(2,1)S(1)}, bf16[2048,256]{1,0:T(8,128)(2,1)}, u32[]{:S(2)}) copy-start(bf16[2048,256]{1,0:T(8,128)(2,1)} %copy-done.3) | copy-start | bytes 3145732
  150.0 51.6 %all-to-all-start.2 = ((bf16[4,16,16384]{2,1,0:T(8,128)(2,1)}), bf16[4,16,16384]{2,1,0:T(8,128)(2,1)S(1)}, u32[]{:S(2)}, u32[]{:S(2)}) async-start(bf16[4,16,16384]{2,1,0:T(8,128)(2,1)} %stack.2), calls=%async_computation.3 | async-start | bytes 4194304 | tf_op jit(solution)/shard_map/all_to_all | solution.py:64
  201.5 1.3 copy-start.2
  213.1 21.2 %copy-start.9 = (s32[16]{0:T(128)S(1)}, s32[16]{0:T(128)}, u32[]{:S(2)}) copy-start(s32[16]{0:T(128)} %param.11) | copy-start | bytes 196
  213.1 21.3 %copy-start.10 = (s32[16]{0:T(128)S(1)}, s32[16]{0:T(128)}, u32[]{:S(2)}) copy-start(s32[16]{0:T(128)} %param.10) | copy-start | bytes 196
  213.1 22.2 %copy-start.1 = (f32[96,128]{1,0:T(8,128)S(1)}, f32[96,128]{1,0:T(8,128)}, u32[]{:S(2)}) copy-start(f32[96,128]{1,0:T(8,128)} %param.12) | copy-start | bytes 147460
Sparse Core Ops, SparseCore 0:
  18.4 46.5 reduce-scatter.1
